TPU v7x, 256 devices: a whole 4x4x8 slice. The times are simulated.
256 devices in a mesh: ctx: 32 (over y, z), head: 8 (over x, core).
Axes of the slice: x: 4, y: 4, z: 8, core: 2. Of those that a mesh axis runs over, the one named last changes fastest.
Arguments:
- queries: bfloat16 [4096, 4096], P('ctx', 'head'), may hold values from -30 to 30
- key_proj: bfloat16 [4096, 1024], P('ctx', 'head'), may hold values from -6 to 6
- value_proj: bfloat16 [4096, 1024], P('ctx', 'head'), may hold values from -6 to 6
- lengths: int32 [32], replicated, may hold values from 1 to 2048, 4096 in all
- out_weight: bfloat16 [4096, 8192], P(None, 'head'), may hold values from -0.09375 to 0.09375
Outputs:
- mixed_out: bfloat16 [4096, 8192], P('ctx', 'head')
Inputs may be any that keep to these rules, and one draw needn't show every extreme that they name: Document lengths in pack order; they sum to 4096 and the longest is exactly 2048.
All inputs are finite; a program needn't handle non-finite values.
Results may differ from a plain program's by a relative error of at most 0.005.
The roundings to bfloat16 on the way count: a program that leaves them out, or rounds other values in their place, can miss the bound.
Values may be sent and summed in bfloat16 or wider, within the bound.
No kernel may reach another device: no remote copies, remote signals or barrier semaphores. Data moves between devices by JAX's collectives and lax.ppermute only.
A program may use at most 64 MiB of HBM per device.

v0:
```python
import jax
import jax.numpy as jnp
from jax import lax
from jax.sharding import PartitionSpec as P

HD = 128
rope_theta = 500000.0


def doc_starts(lengths, positions):
    doc_ends = jnp.cumsum(lengths)
    picked = jnp.where(doc_ends[None, :] <= positions[:, None], lengths[None, :], 0)
    return jnp.sum(picked, axis=1)


def rotary(projected, offsets, head_dim):
    token_count = projected.shape[0]
    heads_grid = projected.astype(jnp.float32).reshape(token_count, -1, head_dim)
    half_dim = head_dim // 2
    inverse = rope_theta ** (-2.0 * jnp.arange(half_dim).astype(jnp.float32) / head_dim)
    angles = offsets.astype(jnp.float32)[:, None] * inverse[None, :]
    cosine = jnp.cos(angles)[:, None, :]
    sine_part = jnp.sin(angles)[:, None, :]
    first_half = heads_grid[..., :half_dim]
    second_half = heads_grid[..., half_dim:]
    rotated = jnp.concatenate(
        [
            first_half * cosine - second_half * sine_part,
            second_half * cosine + first_half * sine_part,
        ],
        axis=-1,
    )
    return rotated.reshape(token_count, -1).astype(jnp.bfloat16)


def on_device(queries, key_proj, value_proj, lengths, out_weight):
    tok_rows = queries.shape[0]
    kv_local = key_proj.shape[1] // HD
    query_group = queries.shape[1] // key_proj.shape[1]
    first_row = lax.axis_index("ctx") * tok_rows
    positions = first_row + jnp.arange(tok_rows, dtype=jnp.int32)
    starts = doc_starts(lengths, positions)
    offsets = positions - starts
    q_rot = rotary(queries, offsets, HD).reshape(tok_rows, kv_local, query_group, HD)
    k_rot = rotary(key_proj, offsets, HD)
    lowest = starts[0]
    initial = (
        jnp.full((kv_local, query_group, tok_rows), -1e30, jnp.float32),
        jnp.zeros((kv_local, query_group, tok_rows), jnp.float32),
        jnp.zeros((kv_local, query_group, tok_rows, HD), jnp.float32),
    )
    begin_row = jnp.int32(0)
    key_part = lax.all_gather(k_rot, "ctx", axis=0, tiled=True)
    value_part = lax.all_gather(value_proj, "ctx", axis=0, tiled=True)
    key_count = key_part.shape[0]

    def update(state):
        running_max, running_sum, weighted = state
        key_block = key_part.reshape(key_count, kv_local, HD)
        value_block = value_part.reshape(key_count, kv_local, HD)
        scores = jnp.einsum(
            "tkgd,nkd->kgtn", q_rot, key_block, preferred_element_type=jnp.float32
        ) / jnp.sqrt(jnp.float32(HD))
        key_pos = jnp.arange(key_count, dtype=jnp.int32)
        allowed = (key_pos[None, :] <= positions[:, None]) & (key_pos[None, :] >= starts[:, None])
        scores = jnp.where(allowed, scores, -1e30)
        new_max = jnp.maximum(running_max, jnp.max(scores, axis=-1))
        weights = jnp.where(allowed, jnp.exp(scores - new_max[..., None]), 0.0)
        new_sum = jnp.sum(weights, axis=-1)
        product = jnp.einsum(
            "kgtn,nkd->kgtd",
            weights.astype(jnp.bfloat16),
            value_block,
            preferred_element_type=jnp.float32,
        )
        return (new_max, new_sum, product)

    needed = (begin_row <= first_row + tok_rows - 1) & (begin_row + key_count - 1 >= lowest)
    state = lax.cond(needed, update, lambda state: state, initial)
    running_max, running_sum, weighted = state
    normed = (weighted / running_sum[..., None]).astype(jnp.bfloat16)
    attended = jnp.transpose(normed, (2, 0, 1, 3)).reshape(tok_rows, kv_local * query_group * HD)
    mixed_out = jnp.dot(
        lax.all_gather(attended, "head", axis=1, tiled=True),
        out_weight,
        preferred_element_type=jnp.float32,
    )
    return mixed_out.astype(jnp.bfloat16)


def solution(mesh):
    placed = (P("ctx", "head"), P("ctx", "head"), P("ctx", "head"), P(), P(None, "head"))
    return jax.shard_map(
        on_device, mesh=mesh, in_specs=placed, out_specs=P("ctx", "head"), check_vma=False
    )
```

profile of v0, /device:TPU:1, one launch (start us, length us, event | category | flops | bytes accessed | tf_op | source)
XLA Modules:
  0.0 206.3 jit_solution(5268036091979652018)
XLA Ops:
  6.5 0.7 all-gather.5.cloned.1.call-update
  7.3 0.0 all-gather.9.cloned.1.call-start
  7.3 0.7 copy.19
  8.0 0.1 reduce-window.8
  8.1 0.1 reduce.2
  8.2 0.9 copy.21
  9.1 0.7 select_reduce_fusion
  9.9 0.2 fusion.23
  10.1 0.6 pad_maximum_fusion.1
  10.7 0.0 all-gather.9.cloned.1.call-update
  10.7 0.0 all-gather.7.cloned.1.call-start
  10.8 1.0 copy.20
  11.9 0.2 multiply_cosine_fusion.1
  12.2 72.9 %all-gather.5.cloned.1.call-done = bf16[4096,128]{1,0:T(8,128)(2,1)} async-done(((bf16[128,128]{1,0:T(8,128)(2,1)}), bf16[4096,128]{1,0:T(8,128)(2,1)}) %all-gather.5.cloned.1.call-update) | async-done | bytes 1048592 | tf_op jit(solution)/shard_map/all_gather | solution.py:54
  85.0 71.6 %all-gather.9.cloned.1.call-done = bf16[4096,1,128]{0,2,1:T(8,128)(2,1)} async-done(((bf16[128,1,128]{0,2,1:T(8,128)(2,1)}), bf16[4096,1,128]{0,2,1:T(8,128)(2,1)}) %all-gather.9.cloned.1.call-update) | async-done | bytes 1048592 | tf_op jit(solution)/shard_map/all_gather | solution.py:53
  156.6 7.3 %conditional.1 = (f32[1,4,128]{2,1,0:T(4,128)S(1)}, f32[1,4,128,128]{2,3,1,0:T(8,128)S(1)}) conditional(s32[]{:T(128)} %convert_element_type.42, () %tuple.13, (s32[]{:T(128)}, s32[128]{0:T(128)S(1)}, s32[128]{0:T(128)S(1)}, bf16[128,4,128]{0,2,1:T(8,128)(2,1)S(1)}, bf16[4096,128]{0,1:T(8,128)(2,1)}, /*index=5*/bf16[4096,128]{1,0:T(8,128)(2,1)}) %tuple.32), branch_computations={%region_2.3_spmd, %region_3.6_spmd} | conditional | flops 1102577280 | bytes 34224176 | solution.py:79
  156.6 0.1 copy.22
  156.8 0.5 fusion.7
  157.3 2.6 %fusion = (f32[4,128]{1,0:T(4,128)S(1)}, f32[4096,128,4]{1,0,2:T(8,128)S(1)}) fusion(pred[128,4096]{0,1:T(8,128)(4,1)S(1)} %fusion.7, bf16[128,4,128]{2,0,1:T(8,128)(2,1)S(1)} %copy.22, bf16[4096,128]{0,1:T(8,128)(2,1)} %get-tuple-element.47), kind=kOutput, calls=%fused_computation.2 | convolution fusion | flops 543161856 | bytes 10094592 | tf_op jit(solution)/shard_map/cond/branch_1_fun/tkgd,nkd->kgtn/dot_general | solution.py:61
  159.9 2.0 fusion.8
  161.8 2.1 %fusion.2 = f32[4,128]{1,0:T(4,128)S(1)} fusion(f32[4096,128,4]{1,0,2:T(8,128)S(1)} %get-tuple-element.51, f32[4,128]{1,0:T(4,128)S(1)} %broadcast_maximum_fusion, pred[128,4096]{0,1:T(8,128)(4,1)S(1)} %fusion.7), kind=kLoop, calls=%fused_computation.4 | loop fusion | flops 10485248 | bytes 8916992 | tf_op jit(solution)/shard_map/cond/branch_1_fun/reduce_sum | solution.py:69
  163.9 0.7 divide_convert_fusion
  164.6 29.4 %all-gather.7.cloned.1.call-done = bf16[128,4096]{0,1:T(8,128)(2,1)} async-done(((bf16[128,512]{0,1:T(8,128)(2,1)}), bf16[128,4096]{0,1:T(8,128)(2,1)}) %all-gather.7.cloned.1.call-update) | async-done | bytes 1048592 | tf_op jit(solution)/shard_map/all_gather | solution.py:84
  194.1 5.7 %convolution_convert_fusion = bf16[128,1024]{1,0:T(8,128)(2,1)} fusion(bf16[128,4096]{0,1:T(8,128)(2,1)} %all-gather.7.cloned.1.call-done, bf16[4096,1024]{1,0:T(8,128)(2,1)} %param.11), kind=kOutput, calls=%fused_computation.21 | convolution fusion | flops 1073872896 | bytes 9699328 | tf_op jit(solution)/shard_map/dot_general | solution.py:83
  (14 shorter events, 0.1 us)
Async XLA Ops:
  6.5 78.5 %all-gather.5.cloned.1.call-start = ((), (), s32[]{:S(2)}) async-start(), calls=%async_computation | async-start | bytes 1081344 | tf_op jit(solution)/shard_map/all_gather | solution.py:54
  7.3 149.4 %all-gather.9.cloned.1.call-start = ((), (), s32[]{:S(2)}) async-start(), calls=%async_computation.2 | async-start | bytes 1081344 | tf_op jit(solution)/shard_map/all_gather | solution.py:53
  10.7 183.3 %all-gather.7.cloned.1.call-start = ((), (), s32[]{:S(2)}) async-start(), calls=%async_computation.1 | async-start | bytes 1179648 | tf_op jit(solution)/shard_map/all_gather | solution.py:84
  156.6 3.2 %copy-start = (bf16[4096,128]{1,0:T(8,128)(2,1)S(1)}, bf16[4096,128]{1,0:T(8,128)(2,1)}, u32[]{:S(2)}) copy-start(bf16[4096,128]{1,0:T(8,128)(2,1)} %get-tuple-element.26) | copy-start | bytes 3145732 | tf_op jit(solution)/shard_map/cond
Sparse Core Ops, SparseCore 0:
  9.9 75.0 all-gather.4
  87.5 69.0 all-gather.8
  164.8 29.2 all-gather.6
where the time goes:
time: 207 us; the launch traced here: 206 us
  waiting for transfers between devices  175 us (85%)
  between operations  13.2 us (6%)
  matrix products  10.3 us (5%)
  other arithmetic  5.29 us (3%)
  local copies, waits for them, and re-layouts  2.76 us (1%)
    all_gather x1, waiting for transfers between devices, on_device(): value_part = lax.all_gather(value_proj, 'ctx', axis=0, tiled=True)  72.9 us
    all_gather x1, waiting for transfers between devices, on_device(): key_part = lax.all_gather(k_rot, 'ctx', axis=0, tiled=True)  71.6 us
    all_gather x1, waiting for transfers between devices, on_device(): lax.all_gather(attended, 'head', axis=1, tiled=True)  29.4 us
    dot_general x1, matrix products, on_device(): jnp.dot(lax.all_gather(attended, 'head', axis=1, tiled=True), out_weight,...  5.7 us
  transfers between devices with their start and end apart: 3, of which 3 were waited for; matrix products, arithmetic and copies ran while one was open for 2% of the time, Pallas kernels for 0%

commit v1 on v0

--- a/solution.py
+++ b/solution.py
@@ -51,7 +51,11 @@
     )
     begin_row = jnp.int32(0)
     key_part = lax.all_gather(k_rot, "ctx", axis=0, tiled=True)
-    value_part = lax.all_gather(value_proj, "ctx", axis=0, tiled=True)
+    desk_produce = lambda field_in: jnp.concatenate(
+        lax.all_to_all(jnp.stack([field_in for _ in range(lax.axis_size("ctx"))]), "ctx", 0, 0),
+        axis=0,
+    )
+    value_part = desk_produce(value_proj)
     key_count = key_part.shape[0]
 
     def update(state):

time: 207 us -> 134 us (0.65)
  waiting for transfers between devices: 175 us -> 87.4 us
  starting transfers between devices: 0.08 us -> 12.1 us
    all_gather x1 -> x0, waiting for transfers between devices: 72.9 us -> none  [on_device(): value_part = lax.all_gather(value_proj, 'ctx', axis=0, tiled=True)]
    all_gather x1, waiting for transfers between devices: 71.6 us -> 57.9 us  [on_device(): key_part = lax.all_gather(k_rot, 'ctx', axis=0, tiled=True)]
    all_to_all x0 -> x1, starting transfers between devices: none -> 12 us  [on_device(): lax.all_to_all(jnp.stack([field_in for _ in range(lax.axis_size('ctx'))])...]
  transfers between devices with their start and end apart: 3 -> 3, of which waited for: 3 -> 2; matrix products, arithmetic and copies ran while one was open for 2% -> 2% of each run, Pallas kernels for 0% -> 0%
where the time goes in v1:
time: 134 us; the launch traced here: 133 us
  waiting for transfers between devices  87.4 us (65%)
  between operations  13.5 us (10%)
  starting transfers between devices  12.1 us (9%)
  matrix products  10.2 us (8%)
  other arithmetic  5.29 us (4%)
  local copies, waits for them, and re-layouts  4.79 us (4%)
    all_gather x1, waiting for transfers between devices, on_device(): key_part = lax.all_gather(k_rot, 'ctx', axis=0, tiled=True)  57.9 us
    all_gather x1, waiting for transfers between devices, on_device(): lax.all_gather(attended, 'head', axis=1, tiled=True)  29.4 us
    all_to_all x1, starting transfers between devices, on_device(): lax.all_to_all(jnp.stack([field_in for _ in range(lax.axis_size('ctx'))])...  12 us
    dot_general x1, matrix products, on_device(): jnp.dot(lax.all_gather(attended, 'head', axis=1, tiled=True), out_weight,...  5.7 us
  transfers between devices with their start and end apart: 3, of which 2 were waited for; matrix products, arithmetic and copies ran while one was open for 2% of the time, Pallas kernels for 0%

profile of v1, /device:TPU:1, one launch (start us, length us, event | category | flops | bytes accessed | tf_op | source)
XLA Modules:
  0.0 133.3 jit_solution(1358570965065763114)
XLA Ops:
  6.5 0.7 copy.19
  7.3 0.1 reduce-window.8
  7.3 0.1 reduce.2
  7.5 0.7 select_reduce_fusion
  8.2 0.9 copy.21
  9.1 0.2 fusion.22
  9.3 0.6 pad_maximum_fusion.1
  9.9 0.0 all-gather.6.cloned.1.call-update
  10.0 2.0 %stack.2 = bf16[32,128,128]{2,1,0:T(8,128)(2,1)} broadcast(bf16[128,128]{1,0:T(8,128)(2,1)} %param.9), dimensions={1,2} | broadcast | bytes 1081344 | tf_op jit(solution)/shard_map/stack | solution.py:55
  12.0 12.0 %all-to-all-start = ((bf16[32,128,128]{2,1,0:T(8,128)(2,1)}), bf16[32,128,128]{2,1,0:T(8,128)(2,1)S(1)}, u32[]{:S(2)}, u32[]{:S(2)}) async-start(bf16[32,128,128]{2,1,0:T(8,128)(2,1)} %stack.2), calls=%async_computation | async-start | bytes 2097152 | tf_op jit(solution)/shard_map/all_to_all | solution.py:55
  24.0 0.0 all-gather.4.cloned.1.call-start
  24.1 1.0 copy.20
  25.2 0.2 multiply_cosine_fusion.1
  25.4 57.9 %all-gather.6.cloned.1.call-done = bf16[4096,1,128]{0,2,1:T(8,128)(2,1)} async-done(((bf16[128,1,128]{0,2,1:T(8,128)(2,1)}), bf16[4096,1,128]{0,2,1:T(8,128)(2,1)}) %all-gather.6.cloned.1.call-update) | async-done | bytes 1048592 | tf_op jit(solution)/shard_map/all_gather | solution.py:53
  83.4 7.3 %conditional.1 = (f32[1,4,128]{2,1,0:T(4,128)S(1)}, f32[1,4,128,128]{2,3,1,0:T(8,128)S(1)}) conditional(s32[]{:T(128)} %convert_element_type.42, () %tuple.13, (s32[]{:T(128)}, s32[128]{0:T(128)S(1)}, s32[128]{0:T(128)S(1)}, bf16[128,4,128]{0,2,1:T(8,128)(2,1)S(1)}, bf16[4096,128]{0,1:T(8,128)(2,1)}, ...), branch_computations={%region_2.3_spmd, %region_3.6_spmd} | conditional | flops 1102577280 | bytes 30029844 | solution.py:83
  83.4 0.1 copy.22
  83.5 0.5 fusion.7
  84.0 2.6 %fusion = (f32[4,128]{1,0:T(4,128)S(1)}, f32[4096,128,4]{1,0,2:T(8,128)S(1)}) fusion(pred[128,4096]{0,1:T(8,128)(4,1)S(1)} %fusion.7, bf16[128,4,128]{2,0,1:T(8,128)(2,1)S(1)} %copy.22, bf16[4096,128]{0,1:T(8,128)(2,1)} %get-tuple-element.47), kind=kOutput, calls=%fused_computation.2 | convolution fusion | flops 543161856 | bytes 10094592 | tf_op jit(solution)/shard_map/cond/branch_1_fun/tkgd,nkd->kgtn/dot_general | solution.py:65
  86.6 1.9 %fusion.8 = f32[1,4,128,128]{2,3,1,0:T(8,128)S(1)} fusion(bf16[4096,128,1]{1,0,2:T(8,128)(2,1)S(1)} %bitcast.51, f32[4096,128,4]{1,0,2:T(8,128)S(1)} %get-tuple-element.51, f32[4,128]{1,0:T(4,128)S(1)} %broadcast_maximum_fusion, pred[128,4096]{0,1:T(8,128)(4,1)S(1)} %fusion.7), kind=kOutput, calls=%fused_computation.11 | convolution fusion | flops 547356672 | bytes 10225664 | tf_op jit(solution)/shard_map/cond/branch_1_fun/kgtn,nkd->kgtd/dot_general | solution.py:74
  88.5 2.1 %fusion.2 = f32[4,128]{1,0:T(4,128)S(1)} fusion(f32[4096,128,4]{1,0,2:T(8,128)S(1)} %get-tuple-element.51, f32[4,128]{1,0:T(4,128)S(1)} %broadcast_maximum_fusion, pred[128,4096]{0,1:T(8,128)(4,1)S(1)} %fusion.7), kind=kLoop, calls=%fused_computation.4 | loop fusion | flops 10485248 | bytes 8916992 | tf_op jit(solution)/shard_map/cond/branch_1_fun/reduce_sum | solution.py:73
  90.6 0.7 divide_convert_fusion
  91.3 0.0 all-gather.4.cloned.1.call-update
  91.3 29.4 %all-gather.4.cloned.1.call-done = bf16[128,4096]{0,1:T(8,128)(2,1)} async-done(((bf16[128,512]{0,1:T(8,128)(2,1)}), bf16[128,4096]{0,1:T(8,128)(2,1)}) %all-gather.4.cloned.1.call-update) | async-done | bytes 1048592 | tf_op jit(solution)/shard_map/all_gather | solution.py:88
  120.8 5.7 %convolution_convert_fusion = bf16[128,1024]{1,0:T(8,128)(2,1)} fusion(bf16[128,4096]{0,1:T(8,128)(2,1)} %all-gather.4.cloned.1.call-done, bf16[4096,1024]{1,0:T(8,128)(2,1)} %param.11), kind=kOutput, calls=%fused_computation.20 | convolution fusion | flops 1073872896 | bytes 9699328 | tf_op jit(solution)/shard_map/dot_general | solution.py:87
  (12 shorter events, 0.1 us)
Async XLA Ops:
  6.5 76.8 %all-gather.6.cloned.1.call-start = ((), (), s32[]{:S(2)}) async-start(), calls=%async_computation.2 | async-start | bytes 1081344 | tf_op jit(solution)/shard_map/all_gather | solution.py:53
  12.0 71.4 %all-to-all-start = ((bf16[32,128,128]{2,1,0:T(8,128)(2,1)}), bf16[32,128,128]{2,1,0:T(8,128)(2,1)S(1)}, u32[]{:S(2)}, u32[]{:S(2)}) async-start(bf16[32,128,128]{2,1,0:T(8,128)(2,1)} %stack.2), calls=%async_computation | async-start | bytes 2097152 | tf_op jit(solution)/shard_map/all_to_all | solution.py:55
  24.0 96.7 %all-gather.4.cloned.1.call-start = ((), (), s32[]{:S(2)}) async-start(), calls=%async_computation.1 | async-start | bytes 1179648 | tf_op jit(solution)/shard_map/all_gather | solution.py:88
Sparse Core Ops, SparseCore 0:
  10.1 73.2 all-gather.5
  91.4 29.2 all-gather.3
